TPU v7x, 256 devices: a whole 4x4x8 slice. The times are simulated.
256 devices in a mesh: replica: 16 (over y_lo, x, core), fsdp: 16 (over z, y_hi).
Axes of the slice: x: 4, y: 4 (y_hi: 2, y_lo: 2; y = y_hi * 2 + y_lo), z: 8, core: 2. Of those that a mesh axis runs over, the one named last changes fastest.
Arguments:
- activations: bfloat16 [65536, 8192], P(('replica', 'fsdp')), may hold values from -6 to 6
- cotangent: bfloat16 [65536, 512], P(('replica', 'fsdp')), may hold values from -12288 to 12288
- labels: int32 [65536], P(('replica', 'fsdp')), may hold values from -1 to 128255, as said below
- local_weight: float32 [16, 8192, 512], P('replica', 'fsdp'), may hold values from -4.5 to 4.5
- first_moment: bfloat16 [16, 8192, 512], P('replica', 'fsdp'), may hold values from -1.75 to 1.75
- second_moment: bfloat16 [16, 8192, 512], P('replica', 'fsdp'), may hold values from 0.019897461 to 2
- anchor_weight: float32 [8192, 512], P('fsdp'), may hold values from -4 to 4
- outer_state: float32 [8192, 512], P('fsdp'), may hold values from -1.75 to 1.75
Outputs:
- input_grad: bfloat16 [65536, 8192], P(('replica', 'fsdp'))
- new_anchor: float32 [8192, 512], P('fsdp')
- new_state: float32 [8192, 512], P('fsdp')
- new_first: bfloat16 [16, 8192, 512], P('replica', 'fsdp')
- new_second: bfloat16 [16, 8192, 512], P('replica', 'fsdp')
Inputs may be any that keep to these rules, and one draw needn't show every extreme that they name: `labels`: each worker's tokens begin with a prompt of at least 512 tokens, labelled -1, and all later tokens carry ids of 0 to 128255; at least 512 of them do.
All inputs are finite; a program needn't handle non-finite values.
Results may differ from a plain program's by a relative error of at most 0.0059.
Values may be sent and summed in bfloat16 or wider, within the bound.
No kernel may reach another device: no remote copies, remote signals or barrier semaphores. Data moves between devices by JAX's collectives and lax.ppermute only.
A program may use at most 128 MiB of HBM per device.

v0:
```python
import jax
import jax.numpy as jnp
from jax import lax
from jax.sharding import PartitionSpec as P

D = 8192
norm_eps = 1e-05
beta_first = 0.9
beta_second = 0.95
adam_eps = 1e-08
weight_decay = 0.1
inner_rate = 0.1
outer_rate = 0.7
outer_momentum = 0.9


def contract_last(left, right):
    return lax.dot_general(
        left, right, (((1,), (1,)), ((), ())), preferred_element_type=jnp.float32
    )


def contract_first(left, right):
    return lax.dot_general(
        left, right, (((0,), (0,)), ((), ())), preferred_element_type=jnp.float32
    )


def per_device(
    activations,
    cotangent,
    labels,
    local_weight,
    first_moment,
    second_moment,
    anchor_weight,
    outer_state,
):
    width_scale = D ** (-0.5)
    weight_shard = local_weight[0]
    weight_low = weight_shard.astype(jnp.bfloat16)
    answer = (labels >= 0).astype(jnp.float32)
    values = activations.astype(jnp.float32)
    inverse = lax.rsqrt(jnp.mean(values * values, axis=1, keepdims=True) + norm_eps)
    normed = values * inverse
    normed_low = normed.astype(jnp.bfloat16)
    answers = lax.psum(jnp.sum(answer), "fsdp")
    scaled = (cotangent.astype(jnp.float32) * answer[:, None] / answers).astype(jnp.bfloat16)
    feature_grad = width_scale * contract_last(
        scaled, lax.all_gather(weight_low, "fsdp", axis=0, tiled=True)
    )
    projected = jnp.mean(feature_grad * normed, axis=1, keepdims=True)
    input_grad = (inverse * (feature_grad - normed * projected)).astype(jnp.bfloat16)
    gradient = lax.psum_scatter(
        (width_scale * contract_first(normed_low, scaled)).astype(jnp.bfloat16),
        "fsdp",
        scatter_dimension=0,
        tiled=True,
    ).astype(jnp.float32)
    first = beta_first * first_moment[0].astype(jnp.float32) + (1.0 - beta_first) * gradient
    second = (
        beta_second * second_moment[0].astype(jnp.float32)
        + (1.0 - beta_second) * gradient * gradient
    )
    stepped = weight_shard - inner_rate * (
        first / (jnp.sqrt(second) + adam_eps) + weight_decay * weight_shard
    )
    pseudo_grad = anchor_weight - stepped
    replicas = lax.axis_size("replica")
    average = lax.psum(pseudo_grad.astype(jnp.bfloat16), "replica").astype(jnp.float32) / replicas
    new_state = outer_momentum * outer_state + average
    new_anchor = anchor_weight - outer_rate * (average + outer_momentum * new_state)
    new_first = first.astype(jnp.bfloat16)[None]
    new_second = second.astype(jnp.bfloat16)[None]
    return (input_grad, new_anchor, new_state, new_first, new_second)


def solution(mesh):
    in_specs = (
        P(("replica", "fsdp"), None),
        P(("replica", "fsdp"), None),
        P(("replica", "fsdp")),
        P("replica", "fsdp", None),
        P("replica", "fsdp", None),
        P("replica", "fsdp", None),
        P("fsdp", None),
        P("fsdp", None),
    )
    out_specs = (
        P(("replica", "fsdp"), None),
        P("fsdp", None),
        P("fsdp", None),
        P("replica", "fsdp", None),
        P("replica", "fsdp", None),
    )
    return jax.shard_map(
        per_device, mesh=mesh, in_specs=in_specs, out_specs=out_specs, check_vma=False
    )
```

profile of v0, /device:TPU:1, one launch (start us, length us, event | category | flops | bytes accessed | tf_op | source)
XLA Modules:
  0.0 511.3 jit_solution(3030680337738197865)
XLA Ops:
  7.2 0.0 all-gather.2.cloned.1.call-start
  7.2 2.1 bitcast_convert_fusion
  9.3 0.0 all-gather.2.cloned.1.call-update
  9.3 0.0 reduce-scatter.2.cloned.1.call-start
  9.4 1.3 fusion.20
  10.7 39.4 %psum.14 = f32[]{:T(128)} all-reduce(f32[]{:T(128)} %fusion.20), channel_id=1, replica_groups=mesh['replica'=16,'fsdp'=16] {'fsdp'}, use_global_device_ids=true, to_apply=%region_2.0 | all-reduce | flops 1 | bytes 8 | tf_op jit(solution)/shard_map/psum | solution.py:47
  50.1 0.7 compare_convert_fusion
  50.8 3.1 fusion.7
  53.9 8.6 %multiply_convert_fusion = bf16[8192,512]{1,0:T(8,128)(2,1)} fusion(bf16[256,8192]{1,0:T(8,128)(2,1)} %param.8, f32[256]{0:T(256)S(1)} %add_rsqrt_fusion, bf16[256,512]{1,0:T(8,128)(2,1)} %param.9, f32[]{:T(128)} %psum.14, f32[256]{0:T(256)S(1)} %compare_convert_fusion), kind=kOutput, calls=%fused_computation | convolution fusion | flops 2162688000 | bytes 12847108 | tf_op jit(solution)/shard_map/dot_general | solution.py:24
  62.5 0.0 copy-start.5
  62.5 0.0 reduce-scatter.2.cloned.1.call-update
  62.5 0.0 copy-start
  62.6 0.0 copy-start.1
  62.6 0.0 copy-start.3
  62.6 0.0 copy-start.4
  62.6 0.0 all-reduce.2.cloned.1.call-start
  62.6 87.0 %all-gather.2.cloned.1.call-done = bf16[8192,512]{1,0:T(8,128)(2,1)} async-done(((bf16[512,512]{1,0:T(8,128)(2,1)}), bf16[8192,512]{1,0:T(8,128)(2,1)}) %all-gather.2.cloned.1.call-update) | async-done | bytes 8388624 | tf_op jit(solution)/shard_map/all_gather | solution.py:50
  149.6 0.0 copy-done.5
  149.6 12.5 %fusion.3 = (f32[256]{0:T(256)S(1)}, f32[256,8192]{1,0:T(8,128)}) fusion(bf16[256,8192]{1,0:T(8,128)(2,1)} %param.8, f32[256]{0:T(256)S(1)} %add_rsqrt_fusion, bf16[8192,512]{1,0:T(8,128)(2,1)} %all-gather.2.cloned.1.call-done, bf16[256,512]{1,0:T(8,128)(2,1)S(1)} %copy-done.5, f32[]{:T(128)} %psum.14, f32[256]{0:T(256)S(1)} %compare_convert_fusion), kind=kOutput, calls=%fused_computation.7 | convolution fusion | flops 2158493440 | bytes 21236740 | tf_op jit(solution)/shard_map/dot_general | solution.py:18
  162.2 210.8 %reduce-scatter.2.cloned.1.call-done = bf16[512,512]{1,0:T(8,128)(2,1)} async-done(((bf16[8192,512]{1,0:T(8,128)(2,1)}), bf16[512,512]{1,0:T(8,128)(2,1)}) %reduce-scatter.2.cloned.1.call-update) | async-done | bytes 524304 | tf_op jit(solution)/shard_map/reduce_scatter | solution.py:54
  373.0 0.0 copy-done
  373.0 0.0 copy-done.1
  373.0 0.0 copy-done.3
  373.0 0.0 copy-done.4
  373.0 3.2 fusion.18
  376.1 0.0 all-reduce.2.cloned.1.call-update
  376.2 0.0 copy-start.2
  376.2 6.9 %fusion.6 = bf16[256,8192]{1,0:T(8,128)(2,1)} fusion(f32[256,8192]{1,0:T(8,128)} %get-tuple-element.11, bf16[256,8192]{1,0:T(8,128)(2,1)} %param.8, f32[256]{0:T(256)S(1)} %broadcast_multiply_fusion, f32[256]{0:T(256)S(1)} %add_rsqrt_fusion), kind=kLoop, calls=%fused_computation.10 | loop fusion | flops 12582912 | bytes 16779264 | tf_op jit(solution)/shard_map/convert_element_type | solution.py:53
  383.1 119.0 %all-reduce.2.cloned.1.call-done = bf16[512,512]{1,0:T(8,128)(2,1)} async-done(((bf16[512,512]{1,0:T(8,128)(2,1)}), bf16[512,512]{1,0:T(8,128)(2,1)}) %all-reduce.2.cloned.1.call-update) | async-done | bytes 524304 | tf_op jit(solution)/shard_map/psum | solution.py:70
  502.1 0.0 copy-done.2
  502.1 2.7 multiply_subtract_fusion
  (2 shorter events, 0.0 us)
Async XLA Ops:
  7.2 142.5 %all-gather.2.cloned.1.call-start = ((), (), s32[]{:S(2)}) async-start(), calls=%async_computation.1 | async-start | bytes 8912896 | tf_op jit(solution)/shard_map/all_gather | solution.py:50
  9.3 363.6 %reduce-scatter.2.cloned.1.call-start = ((), (), s32[]{:S(2)}) async-start(), calls=%async_computation.2 | async-start | bytes 8912896 | tf_op jit(solution)/shard_map/reduce_scatter | solution.py:54
  62.5 87.1 %copy-start.5 = (bf16[256,512]{1,0:T(8,128)(2,1)S(1)}, bf16[256,512]{1,0:T(8,128)(2,1)}, u32[]{:S(2)}) copy-start(bf16[256,512]{1,0:T(8,128)(2,1)} %param.9) | copy-start | bytes 786436
  62.5 310.4 %copy-start = (f32[1,512,512]{2,1,0:T(8,128)S(1)}, f32[1,512,512]{2,1,0:T(8,128)}, u32[]{:S(2)}) copy-start(f32[1,512,512]{2,1,0:T(8,128)} %param.11) | copy-start | bytes 3145732
  62.6 310.4 %copy-start.1 = (f32[512,512]{1,0:T(8,128)S(1)}, f32[512,512]{1,0:T(8,128)}, u32[]{:S(2)}) copy-start(f32[512,512]{1,0:T(8,128)} %param.14) | copy-start | bytes 3145732
  62.6 310.4 %copy-start.3 = (bf16[1,512,512]{2,1,0:T(8,128)(2,1)S(1)}, bf16[1,512,512]{2,1,0:T(8,128)(2,1)}, u32[]{:S(2)}) copy-start(bf16[1,512,512]{2,1,0:T(8,128)(2,1)} %param.13) | copy-start | bytes 1572868
  62.6 310.4 %copy-start.4 = (bf16[1,512,512]{2,1,0:T(8,128)(2,1)S(1)}, bf16[1,512,512]{2,1,0:T(8,128)(2,1)}, u32[]{:S(2)}) copy-start(bf16[1,512,512]{2,1,0:T(8,128)(2,1)} %param.12) | copy-start | bytes 1572868
  62.6 439.5 %all-reduce.2.cloned.1.call-start = ((), (), s32[]{:S(2)}) async-start(), calls=%async_computation.3 | async-start | bytes 1048576 | tf_op jit(solution)/shard_map/psum | solution.py:70
  376.2 125.9 %copy-start.2 = (f32[512,512]{1,0:T(8,128)S(1)}, f32[512,512]{1,0:T(8,128)}, u32[]{:S(2)}) copy-start(f32[512,512]{1,0:T(8,128)} %param.15) | copy-start | bytes 3145732
Sparse Core Ops, SparseCore 0:
  11.1 138.4 all-gather.1
  153.7 219.1 reduce-scatter.1
  376.3 125.7 all-reduce.1
where the time goes:
time: 512 us; the launch traced here: 511 us
  waiting for transfers between devices  417 us (81%)
  blocking collectives  39.4 us (8%)
  matrix products  21.2 us (4%)
  other arithmetic  20 us (4%)
  between operations  13.8 us (3%)
    reduce_scatter x1, waiting for transfers between devices, per_device(): lax.psum_scatter((width_scale * contract_first(normed_low, scaled)).astyp...  211 us
    psum x1, waiting for transfers between devices, per_device(): lax.psum(pseudo_grad.astype(jnp.bfloat16), 'replica').astype(jnp.float32)  119 us
    all_gather x1, waiting for transfers between devices, per_device(): lax.all_gather(weight_low, 'fsdp', axis=0, tiled=True)  87 us
    psum x1, blocking collectives, per_device(): answers = lax.psum(jnp.sum(answer), 'fsdp')  39.4 us
    dot_general x1, matrix products, contract_last(): lax.dot_general(left, right, (((1,), (1,)), ((), ())), preferred_element_...  12.5 us
  transfers between devices with their start and end apart: 3, of which 3 were waited for; matrix products, arithmetic and copies ran while one was open for 6% of the time, Pallas kernels for 0%

commit v1 on v0

--- a/solution.py
+++ b/solution.py
@@ -1,7 +1,9 @@
+import functools
 import jax
 import jax.numpy as jnp
 from jax import lax
 from jax.sharding import PartitionSpec as P
+from jax.lax import all_gather
 
 D = 8192
 norm_eps = 1e-05
@@ -12,6 +14,14 @@
 inner_rate = 0.1
 outer_rate = 0.7
 outer_momentum = 0.9
+
+
+def open_slot_on(patch, link_axis):
+    w1 = all_gather(patch, axis_name=link_axis)
+    return jnp.sum(w1, axis=0)
+
+
+put_quarters_up = functools.partial(open_slot_on, link_axis="replica")
 
 
 def contract_last(left, right):
@@ -67,7 +77,7 @@
     )
     pseudo_grad = anchor_weight - stepped
     replicas = lax.axis_size("replica")
-    average = lax.psum(pseudo_grad.astype(jnp.bfloat16), "replica").astype(jnp.float32) / replicas
+    average = put_quarters_up(pseudo_grad.astype(jnp.bfloat16)).astype(jnp.float32) / replicas
     new_state = outer_momentum * outer_state + average
     new_anchor = anchor_weight - outer_rate * (average + outer_momentum * new_state)
     new_first = first.astype(jnp.bfloat16)[None]

time: 512 us -> 492 us (0.961)
  waiting for transfers between devices: 417 us -> 402 us
    psum x1 -> x0, waiting for transfers between devices: 119 us -> none  [per_device(): lax.psum(pseudo_grad.astype(jnp.bfloat16), 'replica').astype(jnp.float32)]
    all_gather x1, waiting for transfers between devices: 87 us -> 136 us  [per_device(): lax.all_gather(weight_low, 'fsdp', axis=0, tiled=True)]
    all_gather x0 -> x1, waiting for transfers between devices: none -> 43.7 us  [open_slot_on(): w1 = all_gather(patch, axis_name=link_axis)]
    reduce_scatter x1, waiting for transfers between devices: 211 us -> 222 us  [per_device(): lax.psum_scatter((width_scale * contract_first(normed_low, scaled)).astyp...]
  transfers between devices with their start and end apart: 3 -> 3, of which waited for: 3 -> 3; matrix products, arithmetic and copies ran while one was open for 6% -> 3% of each run, Pallas kernels for 0% -> 0%
where the time goes in v1:
time: 492 us
  waiting for transfers between devices  402 us (82%)
  blocking collectives  39.3 us (8%)
  other arithmetic  18.7 us (4%)
  matrix products  16.7 us (3%)
  between operations  13.8 us (3%)
    reduce_scatter x1, waiting for transfers between devices, per_device(): lax.psum_scatter((width_scale * contract_first(normed_low, scaled)).astyp...  222 us
    all_gather x1, waiting for transfers between devices, per_device(): lax.all_gather(weight_low, 'fsdp', axis=0, tiled=True)  136 us
    all_gather x1, waiting for transfers between devices, open_slot_on(): w1 = all_gather(patch, axis_name=link_axis)  43.7 us
    psum x1, blocking collectives, per_device(): answers = lax.psum(jnp.sum(answer), 'fsdp')  39.3 us
  transfers between devices with their start and end apart: 3, of which 3 were waited for; matrix products, arithmetic and copies ran while one was open for 3% of the time, Pallas kernels for 0%

profile of v1, /device:TPU:1, one launch (start us, length us, event | category | flops | bytes accessed | tf_op | source)
XLA Modules:
  0.0 492.0 jit_solution(17385374985229932692)
XLA Ops:
  7.2 0.0 reduce-scatter.2.cloned.1.call-start
  7.2 1.3 fusion.20
  8.5 0.7 compare_convert_fusion
  9.2 39.3 %psum.7 = f32[]{:T(128)} all-reduce(f32[]{:T(128)} %fusion.20), channel_id=1, replica_groups=mesh['replica'=16,'fsdp'=16] {'fsdp'}, use_global_device_ids=true, to_apply=%region_2.0 | all-reduce | flops 1 | bytes 8 | tf_op jit(solution)/shard_map/psum | solution.py:57
  48.5 3.1 fusion.7
  51.6 8.6 %multiply_convert_fusion = bf16[8192,512]{1,0:T(8,128)(2,1)} fusion(bf16[256,8192]{1,0:T(8,128)(2,1)} %param.8, f32[256]{0:T(256)S(1)} %add_rsqrt_fusion, bf16[256,512]{1,0:T(8,128)(2,1)} %param.9, f32[]{:T(128)} %psum.7, f32[256]{0:T(256)S(1)} %compare_convert_fusion), kind=kOutput, calls=%fused_computation | convolution fusion | flops 2162688000 | bytes 12847108 | tf_op jit(solution)/shard_map/dot_general | solution.py:34
  60.2 0.0 copy-start.1
  60.2 0.0 copy-start.2
  60.2 0.0 copy-start.4
  60.2 0.0 copy-start.5
  60.2 0.0 copy-start.6
  60.2 0.0 reduce-scatter.2.cloned.1.call-update
  60.3 0.0 all-gather.4.cloned.1.call-start
  60.3 1.1 copy-done.1
  61.4 0.9 bitcast_convert_fusion
  62.3 0.0 all-gather.4.cloned.1.call-update
  62.3 0.0 all-gather.6.cloned.1.call-start
  62.4 222.1 %reduce-scatter.2.cloned.1.call-done = bf16[512,512]{1,0:T(8,128)(2,1)} async-done(((bf16[8192,512]{1,0:T(8,128)(2,1)}), bf16[512,512]{1,0:T(8,128)(2,1)}) %reduce-scatter.2.cloned.1.call-update) | async-done | bytes 524304 | tf_op jit(solution)/shard_map/reduce_scatter | solution.py:64
  284.4 0.0 copy-done.2
  284.4 0.0 copy-done.4
  284.4 0.0 copy-done.5
  284.4 3.2 fusion.18
  287.6 0.0 all-gather.6.cloned.1.call-update
  287.6 136.4 %all-gather.4.cloned.1.call-done = bf16[8192,512]{1,0:T(8,128)(2,1)} async-done(((bf16[512,512]{1,0:T(8,128)(2,1)}), bf16[8192,512]{1,0:T(8,128)(2,1)}) %all-gather.4.cloned.1.call-update) | async-done | bytes 8388624 | tf_op jit(solution)/shard_map/all_gather | solution.py:60
  424.1 0.0 copy-done.6
  424.1 8.1 %fusion.3 = (f32[256]{0:T(256)S(1)}, f32[256,8192]{1,0:T(8,128)S(1)}) fusion(bf16[256,8192]{1,0:T(8,128)(2,1)} %param.8, f32[256]{0:T(256)S(1)} %add_rsqrt_fusion, bf16[8192,512]{1,0:T(8,128)(2,1)} %all-gather.4.cloned.1.call-done, bf16[256,512]{1,0:T(8,128)(2,1)S(1)} %copy-done.6, f32[]{:T(128)} %psum.7, f32[256]{0:T(256)S(1)} %compare_convert_fusion), kind=kOutput, calls=%fused_computation.7 | convolution fusion | flops 2158493440 | bytes 21236740 | tf_op jit(solution)/shard_map/dot_general | solution.py:28
  432.1 0.0 copy-done
  432.2 3.1 fusion.6
  435.3 43.7 %all-gather.6.cloned.1.call-done = bf16[8192,512]{1,0:T(8,128)(2,1)} async-done(((bf16[512,512]{1,0:T(8,128)(2,1)}), bf16[8192,512]{1,0:T(8,128)(2,1)}) %all-gather.6.cloned.1.call-update) | async-done | bytes 8388624 | tf_op jit(solution)/shard_map/all_gather | solution.py:20
  479.0 4.8 reduce_sum.42
  483.8 0.0 copy-done.3
  483.8 1.6 multiply_subtract_fusion
  (4 shorter events, 0.0 us)
Async XLA Ops:
  7.2 277.3 %reduce-scatter.2.cloned.1.call-start = ((), (), s32[]{:S(2)}) async-start(), calls=%async_computation.2 | async-start | bytes 8912896 | tf_op jit(solution)/shard_map/reduce_scatter | solution.py:64
  60.2 1.2 copy-start.1
  60.2 224.2 %copy-start.2 = (f32[512,512]{1,0:T(8,128)S(1)}, f32[512,512]{1,0:T(8,128)}, u32[]{:S(2)}) copy-start(f32[512,512]{1,0:T(8,128)} %param.14) | copy-start | bytes 3145732
  60.2 224.2 %copy-start.4 = (bf16[1,512,512]{2,1,0:T(8,128)(2,1)S(1)}, bf16[1,512,512]{2,1,0:T(8,128)(2,1)}, u32[]{:S(2)}) copy-start(bf16[1,512,512]{2,1,0:T(8,128)(2,1)} %param.13) | copy-start | bytes 1572868
  60.2 224.2 %copy-start.5 = (bf16[1,512,512]{2,1,0:T(8,128)(2,1)S(1)}, bf16[1,512,512]{2,1,0:T(8,128)(2,1)}, u32[]{:S(2)}) copy-start(bf16[1,512,512]{2,1,0:T(8,128)(2,1)} %param.12) | copy-start | bytes 1572868
  60.2 363.8 %copy-start.6 = (bf16[256,512]{1,0:T(8,128)(2,1)S(1)}, bf16[256,512]{1,0:T(8,128)(2,1)}, u32[]{:S(2)}) copy-start(bf16[256,512]{1,0:T(8,128)(2,1)} %param.9) | copy-start | bytes 786436
  60.3 363.8 %all-gather.4.cloned.1.call-start = ((), (), s32[]{:S(2)}) async-start(), calls=%async_computation.1 | async-start | bytes 8912896 | tf_op jit(solution)/shard_map/all_gather | solution.py:60
  62.3 416.7 %all-gather.6.cloned.1.call-start = ((), (), s32[]{:S(2)}) async-start(), calls=%async_computation.3 | async-start | bytes 8912896 | tf_op jit(solution)/shard_map/all_gather | solution.py:20
  424.1 8.1 %copy-start = (bf16[256,8192]{1,0:T(8,128)(2,1)S(1)}, bf16[256,8192]{1,0:T(8,128)(2,1)}, u32[]{:S(2)}) copy-start(bf16[256,8192]{1,0:T(8,128)(2,1)} %param.8) | copy-start | bytes 12582916
  435.3 48.5 %copy-start.3 = (f32[512,512]{1,0:T(8,128)S(1)}, f32[512,512]{1,0:T(8,128)}, u32[]{:S(2)}) copy-start(f32[512,512]{1,0:T(8,128)} %param.15) | copy-start | bytes 3145732
Sparse Core Ops, SparseCore 0:
  60.4 223.9 reduce-scatter.1
  287.6 136.4 all-gather.3
  426.5 52.4 all-gather.5

commit v2 on v0

--- a/solution.py
+++ b/solution.py
@@ -47,7 +47,16 @@
     answers = lax.psum(jnp.sum(answer), "fsdp")
     scaled = (cotangent.astype(jnp.float32) * answer[:, None] / answers).astype(jnp.bfloat16)
     feature_grad = width_scale * contract_last(
-        scaled, lax.all_gather(weight_low, "fsdp", axis=0, tiled=True)
+        scaled,
+        jnp.concatenate(
+            lax.all_to_all(
+                jnp.stack(lax.axis_size("fsdp") * [weight_low], axis=0),
+                split_axis=0,
+                axis_name="fsdp",
+                concat_axis=0,
+            ),
+            axis=0,
+        ),
     )
     projected = jnp.mean(feature_grad * normed, axis=1, keepdims=True)
     input_grad = (inverse * (feature_grad - normed * projected)).astype(jnp.bfloat16)

time: 512 us -> 616 us (1.20)
  blocking collectives: 39.4 us -> 213 us
  waiting for transfers between devices: 417 us -> 333 us
  starting transfers between devices: 0.12 us -> 12 us
    psum x1, blocking collectives: 39.4 us -> 213 us  [per_device(): answers = lax.psum(jnp.sum(answer), 'fsdp')]
    all_gather x1 -> x0, waiting for transfers between devices: 87 us -> none  [per_device(): lax.all_gather(weight_low, 'fsdp', axis=0, tiled=True)]
    all_to_all x0 -> x1, starting transfers between devices: none -> 11.9 us  [per_device(): lax.all_to_all(jnp.stack(lax.axis_size('fsdp') * [weight_low], axis=0), s...]
  transfers between devices with their start and end apart: 3 -> 3, of which waited for: 3 -> 2; matrix products, arithmetic and copies ran while one was open for 6% -> 5% of each run, Pallas kernels for 0% -> 0%
where the time goes in v2:
time: 616 us
  waiting for transfers between devices  333 us (54%)
  blocking collectives  213 us (35%)
  matrix products  21.3 us (3%)
  other arithmetic  17.8 us (3%)
  between operations  14.1 us (2%)
  starting transfers between devices  12 us (2%)
    reduce_scatter x1, waiting for transfers between devices, per_device(): lax.psum_scatter((width_scale * contract_first(normed_low, scaled)).astyp...  214 us
    psum x1, blocking collectives, per_device(): answers = lax.psum(jnp.sum(answer), 'fsdp')  213 us
    psum x1, waiting for transfers between devices, per_device(): lax.psum(pseudo_grad.astype(jnp.bfloat16), 'replica').astype(jnp.float32)  119 us
    dot_general x1, matrix products, contract_last(): lax.dot_general(left, right, (((1,), (1,)), ((), ())), preferred_element_...  12.8 us
  transfers between devices with their start and end apart: 3, of which 2 were waited for; matrix products, arithmetic and copies ran while one was open for 5% of the time, Pallas kernels for 0%

profile of v2, /device:TPU:1, one launch (start us, length us, event | category | flops | bytes accessed | tf_op | source)
XLA Modules:
  0.0 615.8 jit_solution(220976325014890108)
XLA Ops:
  7.2 1.3 convert_bitcast_fusion
  8.5 4.0 stack.5
  12.5 0.0 copy-start.5
  12.5 0.0 copy-start.6
  12.5 11.9 %all-to-all-start = ((bf16[16,512,512]{2,1,0:T(8,128)(2,1)}), bf16[16,512,512]{2,1,0:T(8,128)(2,1)}, u32[]{:S(2)}, u32[]{:S(2)}) async-start(bf16[16,512,512]{2,1,0:T(8,128)(2,1)} %stack.5), calls=%async_computation | async-start | bytes 16777216 | tf_op jit(solution)/shard_map/all_to_all | solution.py:52
  24.4 0.0 reduce-scatter.2.cloned.1.call-start
  24.5 0.0 copy-done.5
  24.5 0.6 fusion.20
  25.1 3.1 fusion.7
  28.2 213.1 %psum.14 = f32[]{:T(128)} all-reduce(f32[]{:T(128)} %fusion.20), channel_id=1, replica_groups=mesh['replica'=16,'fsdp'=16] {'fsdp'}, use_global_device_ids=true, to_apply=%region_2.0 | all-reduce | flops 1 | bytes 8 | tf_op jit(solution)/shard_map/psum | solution.py:47
  241.3 0.0 copy-done.6
  241.3 8.6 %multiply_convert_fusion = bf16[8192,512]{1,0:T(8,128)(2,1)} fusion(bf16[256,8192]{1,0:T(8,128)(2,1)} %param.8, f32[256]{0:T(256)S(1)} %add_rsqrt_fusion, bf16[256,512]{1,0:T(8,128)(2,1)S(1)} %copy-done.6, f32[]{:T(128)} %psum.14, f32[256]{0:T(256)S(1)} %compare_convert_fusion), kind=kOutput, calls=%fused_computation | convolution fusion | flops 2162688000 | bytes 12847108 | tf_op jit(solution)/shard_map/dot_general | solution.py:24
  249.9 0.0 reduce-scatter.2.cloned.1.call-update
  249.9 0.0 all-reduce.2.cloned.1.call-start
  249.9 0.0 all-to-all-done
  250.0 0.0 copy-start
  250.0 0.0 copy-start.1
  250.0 0.0 copy-start.3
  250.0 0.0 copy-start.4
  250.0 12.8 %fusion.3 = (f32[256]{0:T(256)S(1)}, f32[256,8192]{1,0:T(8,128)}) fusion(bf16[256,8192]{1,0:T(8,128)(2,1)} %param.8, f32[256]{0:T(256)S(1)} %add_rsqrt_fusion, bf16[8192,512]{1,0:T(8,128)(2,1)} %bitcast.1, bf16[256,512]{1,0:T(8,128)(2,1)S(1)} %copy-done.6, f32[]{:T(128)} %psum.14, f32[256]{0:T(256)S(1)} %compare_convert_fusion), kind=kOutput, calls=%fused_computation.7 | convolution fusion | flops 2158493440 | bytes 21236740 | tf_op jit(solution)/shard_map/dot_general | solution.py:18
  262.8 214.4 %reduce-scatter.2.cloned.1.call-done = bf16[512,512]{1,0:T(8,128)(2,1)} async-done(((bf16[8192,512]{1,0:T(8,128)(2,1)}), bf16[512,512]{1,0:T(8,128)(2,1)}) %reduce-scatter.2.cloned.1.call-update) | async-done | bytes 524304 | tf_op jit(solution)/shard_map/reduce_scatter | solution.py:63
  477.2 0.0 copy-done
  477.2 0.0 copy-done.1
  477.2 0.0 copy-done.3
  477.2 0.0 copy-done.4
  477.2 3.2 fusion.18
  480.4 0.0 all-reduce.2.cloned.1.call-update
  480.4 0.0 copy-start.2
  480.4 6.9 %fusion.6 = bf16[256,8192]{1,0:T(8,128)(2,1)} fusion(f32[256,8192]{1,0:T(8,128)} %get-tuple-element.11, bf16[256,8192]{1,0:T(8,128)(2,1)} %param.8, f32[256]{0:T(256)S(1)} %broadcast_multiply_fusion, f32[256]{0:T(256)S(1)} %add_rsqrt_fusion), kind=kLoop, calls=%fused_computation.10 | loop fusion | flops 12582912 | bytes 16779264 | tf_op jit(solution)/shard_map/convert_element_type | solution.py:62
  487.3 118.9 %all-reduce.2.cloned.1.call-done = bf16[512,512]{1,0:T(8,128)(2,1)} async-done(((bf16[512,512]{1,0:T(8,128)(2,1)}), bf16[512,512]{1,0:T(8,128)(2,1)}) %all-reduce.2.cloned.1.call-update) | async-done | bytes 524304 | tf_op jit(solution)/shard_map/psum | solution.py:79
  606.3 0.0 copy-done.2
  606.3 2.7 multiply_subtract_fusion
  (3 shorter events, 0.0 us)
Async XLA Ops:
  12.5 12.0 %copy-start.5 = (s32[256]{0:T(256)S(1)}, s32[256]{0:T(256)}, u32[]{:S(2)}) copy-start(s32[256]{0:T(256)} %param.10) | copy-start | bytes 3076
  12.5 228.8 %copy-start.6 = (bf16[256,512]{1,0:T(8,128)(2,1)S(1)}, bf16[256,512]{1,0:T(8,128)(2,1)}, u32[]{:S(2)}) copy-start(bf16[256,512]{1,0:T(8,128)(2,1)} %param.9) | copy-start | bytes 786436
  12.5 237.5 %all-to-all-start = ((bf16[16,512,512]{2,1,0:T(8,128)(2,1)}), bf16[16,512,512]{2,1,0:T(8,128)(2,1)}, u32[]{:S(2)}, u32[]{:S(2)}) async-start(bf16[16,512,512]{2,1,0:T(8,128)(2,1)} %stack.5), calls=%async_computation | async-start | bytes 16777216 | tf_op jit(solution)/shard_map/all_to_all | solution.py:52
  24.4 452.8 %reduce-scatter.2.cloned.1.call-start = ((), (), s32[]{:S(2)}) async-start(), calls=%async_computation.2 | async-start | bytes 8912896 | tf_op jit(solution)/shard_map/reduce_scatter | solution.py:63
  249.9 356.4 %all-reduce.2.cloned.1.call-start = ((), (), s32[]{:S(2)}) async-start(), calls=%async_computation.3 | async-start | bytes 1048576 | tf_op jit(solution)/shard_map/psum | solution.py:79
  250.0 227.2 %copy-start = (f32[1,512,512]{2,1,0:T(8,128)S(1)}, f32[1,512,512]{2,1,0:T(8,128)}, u32[]{:S(2)}) copy-start(f32[1,512,512]{2,1,0:T(8,128)} %param.11) | copy-start | bytes 3145732
  250.0 227.2 %copy-start.1 = (f32[512,512]{1,0:T(8,128)S(1)}, f32[512,512]{1,0:T(8,128)}, u32[]{:S(2)}) copy-start(f32[512,512]{1,0:T(8,128)} %param.14) | copy-start | bytes 3145732
  250.0 227.2 %copy-start.3 = (bf16[1,512,512]{2,1,0:T(8,128)(2,1)S(1)}, bf16[1,512,512]{2,1,0:T(8,128)(2,1)}, u32[]{:S(2)}) copy-start(bf16[1,512,512]{2,1,0:T(8,128)(2,1)} %param.13) | copy-start | bytes 1572868
  250.0 227.2 %copy-start.4 = (bf16[1,512,512]{2,1,0:T(8,128)(2,1)S(1)}, bf16[1,512,512]{2,1,0:T(8,128)(2,1)}, u32[]{:S(2)}) copy-start(bf16[1,512,512]{2,1,0:T(8,128)(2,1)} %param.12) | copy-start | bytes 1572868
  480.4 125.9 %copy-start.2 = (f32[512,512]{1,0:T(8,128)S(1)}, f32[512,512]{1,0:T(8,128)}, u32[]{:S(2)}) copy-start(f32[512,512]{1,0:T(8,128)} %param.15) | copy-start | bytes 3145732
Sparse Core Ops, SparseCore 0:
  250.0 227.1 reduce-scatter.1
  480.5 125.7 all-reduce.1
